TPU v7x, 512 devices: a whole 4x4x16 slice. The times are simulated.
512 devices in a mesh: dp: 16 (over z), expert: 32 (over y, x, core).
Axes of the slice: x: 4, y: 4, z: 16, core: 2. Of those that a mesh axis runs over, the one named last changes fastest.
Arguments:
- tokens: bfloat16 [65536, 1024], P(('dp', 'expert')), may hold values from -24 to 24
- expert_ids: int32 [65536, 2], P(('dp', 'expert')), may hold values from 0 to 31, all different within a row; in each aligned block of 128 rows (0 to 127, 128 to 255, ...) at most 32 rows name the same one
- route_probs: float32 [65536, 2], P(('dp', 'expert')), may hold values from 0.1 to 1
- w_gate: bfloat16 [32, 1024, 384], P('expert', 'dp'), may hold values from -0.1875 to 0.1875
- w_up: bfloat16 [32, 1024, 384], P('expert', 'dp'), may hold values from -0.1875 to 0.1875
- w_down: bfloat16 [32, 384, 1024], P('expert', None, 'dp'), may hold values from -0.3125 to 0.3125
- grad_out: bfloat16 [65536, 1024], P(('dp', 'expert')), may hold values from -2.5 to 2.5
Outputs:
- mixed_out: bfloat16 [65536, 1024], P(('dp', 'expert'))
- grad_tokens: bfloat16 [65536, 1024], P(('dp', 'expert'))
- grad_probs: float32 [65536, 2], P(('dp', 'expert'))
- grad_w_gate: bfloat16 [32, 1024, 384], P('expert', 'dp')
- grad_w_up: bfloat16 [32, 1024, 384], P('expert', 'dp')
- grad_w_down: bfloat16 [32, 384, 1024], P('expert', None, 'dp')
Inputs may be any that keep to these rules, and one draw needn't show every extreme that they name: `expert_ids`: each row names 2 different experts. Within the rows of one device no expert is named by more than 32 rows, and in every draw some expert is named by exactly 32 rows of some device.
All inputs are finite; a program needn't handle non-finite values.
Results may differ from a plain program's by a relative error of at most 0.017.
Values may be sent and summed in bfloat16 or wider, within the bound.
No kernel may reach another device: no remote copies, remote signals or barrier semaphores. Data moves between devices by JAX's collectives and lax.ppermute only.
A program may use at most 128 MiB of HBM per device.

v0:
```python
import jax
import jax.numpy as jnp
from jax import lax
from jax.sharding import PartitionSpec as P


def route_slots(expert_ids, experts):
    flat_ids = expert_ids.reshape(-1)
    onehot = (flat_ids[:, None] == jnp.arange(experts, dtype=jnp.int32)[None, :]).astype(jnp.int32)
    before = jnp.cumsum(onehot, axis=0) - onehot
    slot_of = jnp.sum(before * onehot, axis=1)
    return (flat_ids, slot_of)


def contract_rows(left_op, right_op):
    return lax.dot_general(
        left_op, right_op, (((0,), (0,)), ((), ())), preferred_element_type=jnp.float32
    )


def contract_cols(left_op, right_op):
    return lax.dot_general(
        left_op, right_op, (((1,), (1,)), ((), ())), preferred_element_type=jnp.float32
    )


def shards(tokens, expert_ids, route_probs, w_gate, w_up, w_down, grad_out):
    senders = lax.axis_size("expert")
    tok_rows, model_width = tokens.shape
    top_count = expert_ids.shape[1]
    hidden_width = w_gate.shape[2]
    capacity = min(tok_rows, 4 * tok_rows * top_count // senders)
    total_rows = senders * capacity
    flat_ids, slot_of = route_slots(expert_ids, senders)
    packed = jnp.concatenate([w_gate[0], w_up[0], w_down[0].T], axis=1)
    whole = lax.all_gather(packed[None], "dp", axis=1, tiled=True)[0]
    gate_up = whole[:, : 2 * hidden_width]
    down_t = whole[:, 2 * hidden_width :]
    grad_wide = grad_out.astype(jnp.float32)
    scaled = (
        (route_probs.T[:, :, None] * grad_wide[None])
        .astype(jnp.bfloat16)
        .reshape(tok_rows * top_count, model_width)
    )
    base = flat_ids * (2 * capacity) + slot_of
    slots = jnp.arange(2 * total_rows, dtype=jnp.int32)[:, None]
    pairs = base.reshape(tok_rows, top_count)
    pick_tok = (slots == pairs[None, :, 0]) | (slots == pairs[None, :, 1])
    pick_grad = slots == (pairs.T.reshape(-1) + capacity)[None, :]
    chooser = jnp.concatenate([pick_tok, pick_grad], axis=1).astype(jnp.bfloat16)
    sources = jnp.concatenate([tokens, scaled], axis=0)
    outgoing = jnp.dot(chooser, sources, preferred_element_type=jnp.float32).astype(jnp.bfloat16)
    arrived = lax.all_to_all(
        outgoing.reshape(senders, 2 * capacity, model_width),
        "expert",
        split_axis=0,
        concat_axis=0,
        tiled=True,
    )
    arrived, whole = lax.optimization_barrier((arrived, whole))
    slot_rows = arrived[:, :capacity].reshape(total_rows, model_width)
    grad_in = arrived[:, capacity:].reshape(total_rows, model_width)
    both_pre = jnp.dot(slot_rows, gate_up, preferred_element_type=jnp.float32)
    gate_pre = both_pre[:, :hidden_width]
    up_pre = both_pre[:, hidden_width:]
    sigmoid_g = jax.nn.sigmoid(gate_pre)
    activated = gate_pre * sigmoid_g
    hidden = (activated * up_pre).astype(jnp.bfloat16)
    back_hidden = jnp.dot(grad_in, down_t, preferred_element_type=jnp.float32)
    back_gate = (back_hidden * up_pre * sigmoid_g * (1.0 + gate_pre * (1.0 - sigmoid_g))).astype(
        jnp.bfloat16
    )
    back_up = (back_hidden * activated).astype(jnp.bfloat16)
    back_both = jnp.concatenate([back_gate, back_up], axis=1)
    grad_terms = jnp.concatenate(
        [
            contract_rows(slot_rows, back_both).astype(jnp.bfloat16),
            contract_rows(grad_in, hidden).astype(jnp.bfloat16),
        ],
        axis=1,
    )
    summed = lax.psum_scatter(grad_terms, "dp", scatter_dimension=0, tiled=True)
    expert_out = contract_cols(hidden, down_t).astype(jnp.bfloat16)
    back_rows = contract_cols(back_both, gate_up).astype(jnp.bfloat16)
    leaving = jnp.concatenate(
        [
            expert_out.reshape(senders, capacity, model_width),
            back_rows.reshape(senders, capacity, model_width),
        ],
        axis=1,
    )
    back_home = lax.all_to_all(leaving, "expert", split_axis=0, concat_axis=0, tiled=True)
    back_home, summed = lax.optimization_barrier((back_home, summed))
    own_place = (flat_ids * capacity + slot_of).reshape(tok_rows, top_count).T.reshape(-1)
    taker = (
        (jnp.arange(total_rows, dtype=jnp.int32)[None, :] == own_place[:, None])
        .astype(jnp.bfloat16)
        .reshape(tok_rows * top_count, senders, capacity)
    )
    picked, back_picked = (
        lax.dot_general(
            taker,
            back_home[:, half * capacity : (half + 1) * capacity],
            (((1, 2), (0, 1)), ((), ())),
            preferred_element_type=jnp.float32,
        ).reshape(top_count, tok_rows, model_width)
        for half in (0, 1)
    )
    probs_k = route_probs.T[:, :, None]
    mixed_out = jnp.sum(probs_k * picked, axis=0).astype(jnp.bfloat16)
    grad_probs = jnp.sum(grad_wide[None] * picked, axis=2).T
    grad_tokens = jnp.sum(back_picked.astype(jnp.float32), axis=0).astype(jnp.bfloat16)
    grad_w_gate = summed[:, :hidden_width][None]
    grad_w_up = summed[:, hidden_width : 2 * hidden_width][None]
    grad_w_down = summed[:, 2 * hidden_width :].T[None]
    return (mixed_out, grad_tokens, grad_probs, grad_w_gate, grad_w_up, grad_w_down)


def solution(mesh):
    placed = (
        P(("dp", "expert"), None),
        P(("dp", "expert"), None),
        P(("dp", "expert"), None),
        P("expert", "dp", None),
        P("expert", "dp", None),
        P("expert", None, "dp"),
        P(("dp", "expert"), None),
    )
    return jax.shard_map(
        shards,
        mesh=mesh,
        in_specs=placed,
        out_specs=(
            P(("dp", "expert"), None),
            P(("dp", "expert"), None),
            P(("dp", "expert"), None),
            P("expert", "dp", None),
            P("expert", "dp", None),
            P("expert", None, "dp"),
        ),
        check_vma=False,
    )
```

profile of v0, /device:TPU:20, one launch (start us, length us, event | category | flops | bytes accessed | tf_op | source)
XLA Modules:
  0.0 189.0 jit_solution(14123776317597047402)
XLA Ops:
  7.2 0.0 copy-start
  7.2 0.0 copy-start.3
  7.2 0.0 all-gather.3.cloned.1.call-start
  7.2 1.6 pad_maximum_fusion.5
  8.8 0.0 all-gather.3.cloned.1.call-update
  8.8 0.0 reduce-scatter.4.cloned.1.call-start
  8.9 0.8 copy.51
  9.7 0.1 eq.98
  9.8 0.1 eq.94
  9.9 0.6 reduce-window.6
  10.5 0.2 slice_reduce_fusion
  10.8 0.1 fusion.40
  10.9 0.1 reduce_sum.39
  11.0 0.1 copy.54
  11.1 0.7 add_bitcast_fusion.1
  11.8 0.3 iota_compare_fusion
  12.1 0.2 fusion.27
  12.4 1.0 convert_element_type.48
  13.4 0.0 copy-done
  13.4 0.1 fusion.26
  13.5 0.0 copy-done.3
  13.5 2.3 %convolution_convert_fusion = bf16[2048,1024]{1,0:T(8,128)(2,1)S(1)} fusion(pred[2048,256]{1,0:T(32,128)(4,1)S(1)} %iota_compare_fusion, pred[2048,128]{1,0:T(32,128)(4,1)S(1)} %fusion.27, bf16[256,1024]{1,0:T(8,128)(2,1)S(1)} %fusion.26, bf16[128,1024]{1,0:T(8,128)(2,1)S(1)} %copy-done.3), kind=kOutput, calls=%fused_computation.1 | convolution fusion | flops 1615069184 | bytes 5767168 | tf_op jit(solution)/shard_map/dot_general | solution.py:52
  15.9 56.1 %all_to_all.10 = bf16[32,64,1024]{2,1,0:T(8,128)(2,1)} all-to-all(bf16[32,64,1024]{2,1,0:T(8,128)(2,1)S(1)} %bitcast.84), channel_id=1, replica_groups=mesh['dp'=16,'expert'=32] {'expert'}, dimensions={0} | all-to-all | bytes 8388608 | tf_op jit(solution)/shard_map/all_to_all | solution.py:53
  72.0 17.1 %all-gather.3.cloned.1.call-done = bf16[1024,1152]{1,0:T(8,128)(2,1)} async-done(((bf16[64,1152]{1,0:T(8,128)(2,1)}), bf16[1024,1152]{1,0:T(8,128)(2,1)}) %all-gather.3.cloned.1.call-update) | async-done | bytes 2359312 | tf_op jit(solution)/shard_map/all_gather | solution.py:36
  89.0 0.0 copy-start.1
  89.0 2.8 %fusion.46 = (bf16[32,32,1024]{2,1,0:T(8,128)(2,1)S(1)}, bf16[32,32,1024]{2,1,0:T(8,128)(2,1)S(1)}) fusion(bf16[32,64,1024]{2,1,0:T(8,128)(2,1)} %all_to_all.10), kind=kLoop, calls=%fused_computation.71 | loop fusion | bytes 8388608 | tf_op jit(solution)/shard_map/slice | solution.py:61
  91.9 0.1 copy-done.1
  92.0 1.9 %fusion.11 = f32[1024,768]{0,1:T(8,128)S(1)} fusion(bf16[1024,1024]{1,0:T(8,128)(2,1)S(1)} %bitcast.85, bf16[1024,1152]{1,0:T(8,128)(2,1)S(1)} %copy-done.1), kind=kOutput, calls=%fused_computation.24 | convolution fusion | flops 1610612736 | bytes 6815744 | tf_op jit(solution)/shard_map/dot_general | solution.py:63
  93.9 1.7 multiply_convert_fusion.1
  95.6 0.0 copy-start.4
  95.6 0.0 copy-start.5
  95.6 0.0 copy-start.7
  95.6 1.0 convolution_convert_fusion.4
  96.6 0.0 copy-done.4
  96.6 0.1 copy-done.5
  96.7 0.3 copy-done.7
  97.0 1.8 convolution_convert_fusion.3
  98.8 0.2 pad_maximum_fusion.1
  99.0 2.5 %copy.61 = bf16[1024,1152]{1,0:T(8,128)(2,1)} copy(bf16[1024,1152]{0,1:T(8,128)(2,1)S(1)} %pad_maximum_fusion.1) | data formatting | bytes 4718592
  101.5 0.0 copy-start.2
  101.5 0.0 reduce-scatter.4.cloned.1.call-update
  101.6 1.6 copy-done.2
  103.2 0.0 copy-start.6
  103.2 0.0 copy-start.8
  103.2 2.6 %convolution_convert_fusion.1 = bf16[1024,1024]{1,0:T(8,128)(2,1)S(1)} fusion(bf16[1024,384]{0,1:T(8,128)(2,1)} %copy-done.4, bf16[1024,1152]{1,0:T(8,128)(2,1)S(1)} %copy-done.2), kind=kOutput, calls=%fused_computation.13 | convolution fusion | flops 806354944 | bytes 3670016 | tf_op jit(solution)/shard_map/dot_general | solution.py:22
  105.8 0.0 copy-done.6
  105.8 0.0 copy-done.8
  105.8 1.9 convolution_convert_fusion.2
  107.7 2.7 %pad_maximum_fusion = bf16[32,64,1024]{2,1,0:T(8,128)(2,1)} fusion(bf16[32,32,1024]{2,1,0:T(8,128)(2,1)S(1)} %bitcast.90, bf16[32,32,1024]{2,1,0:T(8,128)(2,1)S(1)} %bitcast.89), kind=kLoop, calls=%fused_computation | loop fusion | flops 8388608 | bytes 8388608 | tf_op jit(solution)/shard_map/concatenate | solution.py:85
  110.4 7.4 %all-to-all-start.1 = ((bf16[32,64,1024]{2,1,0:T(8,128)(2,1)}), bf16[32,64,1024]{2,1,0:T(8,128)(2,1)}, u32[]{:S(2)}, u32[]{:S(2)}) async-start(bf16[32,64,1024]{2,1,0:T(8,128)(2,1)} %pad_maximum_fusion), calls=%async_computation.1 | async-start | bytes 8388608 | tf_op jit(solution)/shard_map/all_to_all | solution.py:92
  117.8 54.2 %reduce-scatter.4.cloned.1.call-done = bf16[64,1152]{1,0:T(8,128)(2,1)} async-done(((bf16[1024,1152]{1,0:T(8,128)(2,1)}), bf16[64,1152]{1,0:T(8,128)(2,1)}) %reduce-scatter.4.cloned.1.call-update) | async-done | bytes 147472
  172.0 1.1 copy.62
  173.2 0.0 all-to-all-done.1
  173.2 0.7 copy.56
  173.9 0.7 copy.57
  174.6 0.7 copy.58
  175.4 3.3 %fusion.21 = bf16[128,1024]{1,0:T(8,128)(2,1)} fusion(bf16[32,64,1024]{2,1,0:T(8,128)(2,1)} %all-to-all-done.1, s32[2,128]{1,0:T(2,128)S(1)} %get-tuple-element.54, s32[32,32]{1,0:T(8,128)S(1)} %multiply_add_fusion), kind=kOutput, calls=%fused_computation.30 | convolution fusion | flops 537264128 | bytes 2364416 | tf_op jit(solution)/shard_map/dot_general | solution.py:101
  178.7 3.4 %multiply_reduce_fusion = (f32[2,128]{1,0:T(2,128)}, bf16[128,1024]{1,0:T(8,128)(2,1)}) fusion(f32[128,1024]{1,0:T(8,128)S(1)} %convert_element_type.48, f32[2,128]{1,0:T(2,128)S(1)} %bitcast.95, bf16[32,64,1024]{2,1,0:T(8,128)(2,1)} %all-to-all-done.1, s32[2,128]{1,0:T(2,128)S(1)} %get-tuple-element.54, s32[32,32]{1,0:T(8,128)S(1)} %multiply_add_fusion), kind=kOutput, calls=%fused_computation.33 | convolution fusion | flops 538050304 | bytes 2890752 | tf_op jit(solution)/shard_map/dot_general | solution.py:101
  (6 shorter events, 0.1 us)
Async XLA Ops:
  7.2 6.2 %copy-start = (f32[128,2]{0,1:T(2,128)S(1)}, f32[128,2]{0,1:T(2,128)}, u32[]{:S(2)}) copy-start(f32[128,2]{0,1:T(2,128)} %param.9) | copy-start | bytes 3076
  7.2 6.3 %copy-start.3 = (bf16[128,1024]{1,0:T(8,128)(2,1)S(1)}, bf16[128,1024]{1,0:T(8,128)(2,1)}, u32[]{:S(2)}) copy-start(bf16[128,1024]{1,0:T(8,128)(2,1)} %param.7) | copy-start | bytes 786436
  7.2 81.8 %all-gather.3.cloned.1.call-start = ((), (), s32[]{:S(2)}) async-start(), calls=%async_computation.3 | async-start | bytes 2506752 | tf_op jit(solution)/shard_map/all_gather | solution.py:36
  8.8 163.2 %reduce-scatter.4.cloned.1.call-start = ((), (), s32[]{:S(2)}) async-start(), calls=%async_computation.4 | async-start | bytes 2506752
  89.0 2.9 %copy-start.1 = (bf16[1024,1152]{1,0:T(8,128)(2,1)S(1)}, bf16[1024,1152]{1,0:T(8,128)(2,1)}, u32[]{:S(2)}) copy-start(bf16[1024,1152]{1,0:T(8,128)(2,1)} %all-gather.3.cloned.1.call-done) | copy-start | bytes 7077892
  95.6 1.0 copy-start.4
  95.6 1.1 copy-start.5
  95.6 1.4 copy-start.7
  101.5 1.7 copy-start.2
  103.2 2.6 %copy-start.6 = (bf16[1024,384]{0,1:T(8,128)(2,1)S(1)}, bf16[1024,384]{0,1:T(8,128)(2,1)}, u32[]{:S(2)}) copy-start(bf16[1024,384]{0,1:T(8,128)(2,1)} %copy-done.5) | copy-start | bytes 2359300
  103.2 2.6 %copy-start.8 = (bf16[1024,384]{0,1:T(8,128)(2,1)S(1)}, bf16[1024,384]{0,1:T(8,128)(2,1)}, u32[]{:S(2)}) copy-start(bf16[1024,384]{0,1:T(8,128)(2,1)} %copy-done.7) | copy-start | bytes 2359300
  110.4 62.8 %all-to-all-start.1 = ((bf16[32,64,1024]{2,1,0:T(8,128)(2,1)}), bf16[32,64,1024]{2,1,0:T(8,128)(2,1)}, u32[]{:S(2)}, u32[]{:S(2)}) async-start(bf16[32,64,1024]{2,1,0:T(8,128)(2,1)} %pad_maximum_fusion), calls=%async_computation.1 | async-start | bytes 8388608 | tf_op jit(solution)/shard_map/all_to_all | solution.py:92
Sparse Core Ops, SparseCore 0:
  10.7 78.3 all-gather.2
  101.7 70.3 reduce-scatter.3
where the time goes:
time: 189 us
  waiting for transfers between devices  71.4 us (38%)
  blocking collectives  56.1 us (30%)
  matrix products  19.9 us (11%)
  between operations  14.3 us (8%)
  local copies, waits for them, and re-layouts  12.2 us (6%)
  other arithmetic  7.57 us (4%)
  starting transfers between devices  7.52 us (4%)
    all_to_all x1, blocking collectives, shards(): lax.all_to_all(outgoing.reshape(senders, 2 * capacity, model_width), 'exp...  56.1 us
    unnamed x3, waiting for transfers between devices  54.3 us
    all_gather x1, waiting for transfers between devices, shards(): whole = lax.all_gather(packed[None], 'dp', axis=1, tiled=True)[0]  17.1 us
    unnamed x23, local copies, waits for them, and re-layouts  7.6 us
    all_to_all x1, starting transfers between devices, shards(): lax.all_to_all(leaving, 'expert', split_axis=0, concat_axis=0, tiled=True)  7.44 us
    dot_general x2, matrix products, shards(): lax.dot_general(taker, back_home[:, half * capacity:(half + 1) * capacity...  6.76 us
    dot_general x2, matrix products, contract_cols(): lax.dot_general(left_op, right_op, (((1,), (1,)), ((), ())), preferred_el...  4.42 us
  transfers between devices with their start and end apart: 3, of which 2 were waited for; matrix products, arithmetic and copies ran while one was open for 8% of the time, Pallas kernels for 0%

commit v1 on v0

--- a/solution.py
+++ b/solution.py
@@ -33,7 +33,16 @@
     total_rows = senders * capacity
     flat_ids, slot_of = route_slots(expert_ids, senders)
     packed = jnp.concatenate([w_gate[0], w_up[0], w_down[0].T], axis=1)
-    whole = lax.all_gather(packed[None], "dp", axis=1, tiled=True)[0]
+    form_frame_on = lambda along_dim, x0: jnp.concatenate(
+        lax.all_to_all(
+            jnp.stack(lax.axis_size("dp") * [x0], axis=0),
+            axis_name="dp",
+            split_axis=0,
+            concat_axis=0,
+        ),
+        along_dim,
+    )
+    whole = form_frame_on(1, packed[None])[0]
     gate_up = whole[:, : 2 * hidden_width]
     down_t = whole[:, 2 * hidden_width :]
     grad_wide = grad_out.astype(jnp.float32)

time: 189 us -> 296 us (1.57)
  the two profiles are of different devices: /device:TPU:20 before, /device:TPU:2 now
where the time goes in v1:
time: 296 us; the launch traced here: 295 us
  blocking collectives  121 us (41%)
  waiting for transfers between devices  104 us (35%)
  matrix products  21.9 us (7%)
  starting transfers between devices  15.7 us (5%)
  between operations  14.3 us (5%)
  local copies, waits for them, and re-layouts  13.2 us (4%)
  other arithmetic  6.02 us (2%)
    all_to_all x1, blocking collectives, shards(): lax.all_to_all(jnp.stack(lax.axis_size('dp') * [x0], axis=0), axis_name='...  121 us
    unnamed x2, waiting for transfers between devices  52.2 us
    all_to_all x1, waiting for transfers between devices, shards(): lax.all_to_all(outgoing.reshape(senders, 2 * capacity, model_width), 'exp...  51.4 us
    all_to_all x1, starting transfers between devices, shards(): lax.all_to_all(outgoing.reshape(senders, 2 * capacity, model_width), 'exp...  10.5 us
    unnamed x29, local copies, waits for them, and re-layouts  7.52 us
    dot_general x2, matrix products, shards(): lax.dot_general(taker, back_home[:, half * capacity:(half + 1) * capacity...  6.76 us
  transfers between devices with their start and end apart: 3, of which 2 were waited for; matrix products, arithmetic and copies ran while one was open for 3% of the time, Pallas kernels for 0%

profile of v1, /device:TPU:2, one launch (start us, length us, event | category | flops | bytes accessed | tf_op | source)
XLA Modules:
  0.0 295.3 jit_solution(1000982617015560960)
XLA Ops:
  7.2 0.0 copy-start.5
  7.2 0.0 copy-start.6
  7.2 0.8 copy.51
  8.0 0.1 eq.98
  8.2 0.1 eq.94
  8.3 0.6 reduce-window.6
  8.9 0.2 slice_reduce_fusion
  9.1 0.1 fusion.40
  9.2 0.1 reduce_sum.39
  9.4 0.1 copy.54
  9.4 0.7 add_bitcast_fusion.1
  10.2 0.3 iota_compare_fusion
  10.5 1.0 convert_element_type.48
  11.5 0.2 fusion.27
  11.7 0.0 copy-done.5
  11.7 0.1 fusion.26
  11.9 0.0 copy-done.6
  11.9 4.3 %convolution_convert_fusion = bf16[2048,1024]{1,0:T(8,128)(2,1)} fusion(pred[2048,256]{1,0:T(32,128)(4,1)S(1)} %iota_compare_fusion, pred[2048,128]{1,0:T(32,128)(4,1)S(1)} %fusion.27, bf16[256,1024]{1,0:T(8,128)(2,1)S(1)} %fusion.26, bf16[128,1024]{1,0:T(8,128)(2,1)S(1)} %copy-done.6), kind=kOutput, calls=%fused_computation.1 | convolution fusion | flops 1615069184 | bytes 5767168 | tf_op jit(solution)/shard_map/dot_general | solution.py:61
  16.2 0.0 copy-start.2
  16.2 0.0 copy-start.3
  16.2 0.0 copy-start.4
  16.2 10.5 %all-to-all-start = ((bf16[32,64,1024]{2,1,0:T(8,128)(2,1)}), bf16[32,64,1024]{2,1,0:T(8,128)(2,1)}, u32[]{:S(2)}, u32[]{:S(2)}) async-start(bf16[32,64,1024]{2,1,0:T(8,128)(2,1)} %bitcast.85), calls=%async_computation | async-start | bytes 8388608 | tf_op jit(solution)/shard_map/all_to_all | solution.py:62
  26.7 0.0 reduce-scatter.4.cloned.1.call-start
  26.7 0.0 copy-done.2
  26.7 0.0 copy-done.3
  26.8 0.0 copy-done.4
  26.8 51.4 %all-to-all-done = bf16[32,64,1024]{2,1,0:T(8,128)(2,1)} async-done(((bf16[32,64,1024]{2,1,0:T(8,128)(2,1)}), bf16[32,64,1024]{2,1,0:T(8,128)(2,1)}, u32[]{:S(2)}, u32[]{:S(2)}) %all-to-all-start) | async-done | bytes 4194336 | tf_op jit(solution)/shard_map/all_to_all | solution.py:62
  78.2 0.3 stack.3
  78.5 120.7 %all_to_all.15 = bf16[16,1,64,1152]{3,2,1,0:T(8,128)(2,1)S(1)} all-to-all(bf16[16,1,64,1152]{3,2,1,0:T(8,128)(2,1)S(1)} %stack.3), channel_id=1, replica_groups=mesh['dp'=16,'expert'=32] {'dp'}, dimensions={0} | all-to-all | bytes 4718592 | tf_op jit(solution)/shard_map/all_to_all | solution.py:37
  199.1 0.0 copy-start
  199.1 3.5 %fusion.46 = (bf16[32,32,1024]{2,1,0:T(8,128)(2,1)S(1)}, bf16[32,32,1024]{2,1,0:T(8,128)(2,1)S(1)}) fusion(bf16[32,64,1024]{2,1,0:T(8,128)(2,1)} %all-to-all-done), kind=kLoop, calls=%fused_computation.71 | loop fusion | bytes 8388608 | tf_op jit(solution)/shard_map/slice | solution.py:70
  202.7 1.9 fusion.11
  204.6 0.0 copy-done
  204.6 1.7 multiply_convert_fusion.1
  206.3 0.0 copy-start.7
  206.3 0.0 copy-start.8
  206.3 0.0 copy-start.10
  206.3 1.0 convolution_convert_fusion.4
  207.3 0.0 copy-done.7
  207.3 0.1 copy-done.8
  207.4 0.3 copy-done.10
  207.7 1.8 convolution_convert_fusion.3
  209.5 0.2 pad_maximum_fusion.1
  209.7 2.5 copy.61
  212.2 0.0 copy-start.1
  212.2 0.0 reduce-scatter.4.cloned.1.call-update
  212.2 1.6 copy-done.1
  213.9 0.0 copy-start.9
  213.9 0.0 copy-start.11
  213.9 2.6 convolution_convert_fusion.1
  216.5 0.0 copy-done.9
  216.5 0.0 copy-done.11
  216.5 1.9 convolution_convert_fusion.2
  218.3 2.7 pad_maximum_fusion
  221.0 5.2 %all-to-all-start.2 = ((bf16[32,64,1024]{2,1,0:T(8,128)(2,1)}), bf16[32,64,1024]{2,1,0:T(8,128)(2,1)}, u32[]{:S(2)}, u32[]{:S(2)}) async-start(bf16[32,64,1024]{2,1,0:T(8,128)(2,1)} %pad_maximum_fusion), calls=%async_computation.2 | async-start | bytes 8388608 | tf_op jit(solution)/shard_map/all_to_all | solution.py:101
  226.2 52.1 %reduce-scatter.4.cloned.1.call-done = bf16[64,1152]{1,0:T(8,128)(2,1)} async-done(((bf16[1024,1152]{1,0:T(8,128)(2,1)}), bf16[64,1152]{1,0:T(8,128)(2,1)}) %reduce-scatter.4.cloned.1.call-update) | async-done | bytes 147472
  278.4 1.1 copy.62
  279.5 0.0 all-to-all-done.2
  279.5 0.7 copy.56
  280.3 0.7 copy.57
  281.0 0.7 copy.58
  281.7 3.3 %fusion.21 = bf16[128,1024]{1,0:T(8,128)(2,1)} fusion(bf16[32,64,1024]{2,1,0:T(8,128)(2,1)} %all-to-all-done.2, s32[2,128]{1,0:T(2,128)S(1)} %get-tuple-element.54, s32[32,32]{1,0:T(8,128)S(1)} %multiply_add_fusion), kind=kOutput, calls=%fused_computation.30 | convolution fusion | flops 537264128 | bytes 2364416 | tf_op jit(solution)/shard_map/dot_general | solution.py:110
  285.0 3.4 %multiply_reduce_fusion = (f32[2,128]{1,0:T(2,128)}, bf16[128,1024]{1,0:T(8,128)(2,1)}) fusion(f32[128,1024]{1,0:T(8,128)S(1)} %convert_element_type.48, f32[2,128]{1,0:T(2,128)S(1)} %bitcast.100, bf16[32,64,1024]{2,1,0:T(8,128)(2,1)} %all-to-all-done.2, s32[2,128]{1,0:T(2,128)S(1)} %get-tuple-element.54, s32[32,32]{1,0:T(8,128)S(1)} %multiply_add_fusion), kind=kOutput, calls=%fused_computation.33 | convolution fusion | flops 538050304 | bytes 2890752 | tf_op jit(solution)/shard_map/dot_general | solution.py:110
  (7 shorter events, 0.1 us)
Async XLA Ops:
  7.2 4.6 %copy-start.5 = (f32[128,2]{0,1:T(2,128)S(1)}, f32[128,2]{0,1:T(2,128)}, u32[]{:S(2)}) copy-start(f32[128,2]{0,1:T(2,128)} %param.9) | copy-start | bytes 3076
  7.2 4.7 %copy-start.6 = (bf16[128,1024]{1,0:T(8,128)(2,1)S(1)}, bf16[128,1024]{1,0:T(8,128)(2,1)}, u32[]{:S(2)}) copy-start(bf16[128,1024]{1,0:T(8,128)(2,1)} %param.7) | copy-start | bytes 786436
  16.2 10.5 %copy-start.2 = (bf16[1,384,64]{1,2,0:T(8,128)(2,1)S(1)}, bf16[1,384,64]{1,2,0:T(8,128)(2,1)}, u32[]{:S(2)}) copy-start(bf16[1,384,64]{1,2,0:T(8,128)(2,1)} %param.12) | copy-start | bytes 147460
  16.2 10.5 %copy-start.3 = (bf16[1,64,384]{2,1,0:T(8,128)(2,1)S(1)}, bf16[1,64,384]{2,1,0:T(8,128)(2,1)}, u32[]{:S(2)}) copy-start(bf16[1,64,384]{2,1,0:T(8,128)(2,1)} %param.11) | copy-start | bytes 147460
  16.2 10.6 %copy-start.4 = (bf16[1,64,384]{2,1,0:T(8,128)(2,1)S(1)}, bf16[1,64,384]{2,1,0:T(8,128)(2,1)}, u32[]{:S(2)}) copy-start(bf16[1,64,384]{2,1,0:T(8,128)(2,1)} %param.10) | copy-start | bytes 147460
  16.2 62.0 %all-to-all-start = ((bf16[32,64,1024]{2,1,0:T(8,128)(2,1)}), bf16[32,64,1024]{2,1,0:T(8,128)(2,1)}, u32[]{:S(2)}, u32[]{:S(2)}) async-start(bf16[32,64,1024]{2,1,0:T(8,128)(2,1)} %bitcast.85), calls=%async_computation | async-start | bytes 8388608 | tf_op jit(solution)/shard_map/all_to_all | solution.py:62
  26.7 251.7 %reduce-scatter.4.cloned.1.call-start = ((), (), s32[]{:S(2)}) async-start(), calls=%async_computation.4 | async-start | bytes 2506752
  199.1 5.4 %copy-start = (bf16[16,1,64,1152]{3,2,1,0:T(8,128)(2,1)}, bf16[16,1,64,1152]{3,2,1,0:T(8,128)(2,1)S(1)}, u32[]{:S(2)}) copy-start(bf16[16,1,64,1152]{3,2,1,0:T(8,128)(2,1)S(1)} %all_to_all.15) | copy-start | bytes 7077892
  206.3 1.0 copy-start.7
  206.3 1.1 copy-start.8
  206.3 1.4 copy-start.10
  212.2 1.7 copy-start.1
  213.9 2.6 copy-start.9
  213.9 2.6 copy-start.11
  221.0 58.5 %all-to-all-start.2 = ((bf16[32,64,1024]{2,1,0:T(8,128)(2,1)}), bf16[32,64,1024]{2,1,0:T(8,128)(2,1)}, u32[]{:S(2)}, u32[]{:S(2)}) async-start(bf16[32,64,1024]{2,1,0:T(8,128)(2,1)} %pad_maximum_fusion), calls=%async_computation.2 | async-start | bytes 8388608 | tf_op jit(solution)/shard_map/all_to_all | solution.py:101
Sparse Core Ops, SparseCore 0:
  212.4 65.9 reduce-scatter.3
